TPU v7x, 512 devices: a whole 4x8x8 slice. The times are simulated.
512 devices in a mesh: section: 8 (over z_lo, x), fsdp: 64 (over z_hi, y, core).
Axes of the slice: x: 4, y: 8, z: 8 (z_hi: 4, z_lo: 2; z = z_hi * 2 + z_lo), core: 2. Of those that a mesh axis runs over, the one named last changes fastest.
Arguments:
- activations: bfloat16 [10240, 6144], P('fsdp'), may hold values from -36 to 36
- keep: int32 [10240], P('fsdp'), may hold values from 0 to 1, as said below
- gains: bfloat16 [8, 6144], P('section'), may hold values from 0.099609375 to 1.8984375
- up_rows: int32 [8, 192, 2], P('section'), may hold values from 0 to 95
- up_blocks: bfloat16 [8, 384, 4096], P('section', 'fsdp'), may hold values from -0.5 to 0.5
- down_rows: int32 [8, 96, 2], P('section'), may hold values from 0 to 191
- down_blocks: bfloat16 [8, 192, 4096], P('section', 'fsdp'), may hold values from -0.5 to 0.5
Outputs:
- section_out: bfloat16 [8, 10240, 6144], P('section', 'fsdp')
Inputs may be any that keep to these rules, and one draw needn't show every extreme that they name: `keep`: each aligned block of 160 tokens (the tokens of one index of fsdp) holds exactly 128 ones.
All inputs are finite; a program needn't handle non-finite values.
Results may differ from a plain program's by a relative error of at most 0.012.
Values may be sent and summed in bfloat16 or wider, within the bound.
No kernel may reach another device: no remote copies, remote signals or barrier semaphores. Data moves between devices by JAX's collectives and lax.ppermute only.
A program may use at most 128 MiB of HBM per device.

v0:
```python
import jax
import jax.numpy as jnp
from jax import lax
from jax.sharding import Mesh
from jax.sharding import PartitionSpec as P

BLK = 64
UP_DEPTH = 2
DOWN_DEPTH = 2
KEEP_DEV = 128
SEC = ("zl", "x")
FS = ("zh", "y", "c")


def from_behind(value, axis, steps):
    count = lax.axis_size(axis)
    initial, last = (max(0, -steps), min(count, count - steps))
    return lax.ppermute(value, axis, [(source, source + steps) for source in range(initial, last)])


def exchange_zh(part):
    count = lax.axis_size("zh")
    own = lax.axis_index("zh")
    got = [part]
    for shift in range(1, count):
        got.append(lax.ppermute(part, "zh", [(i, (i + shift) % count) for i in range(count)]))
    stacked = jnp.stack(got)
    order = (own - jnp.arange(count, dtype=jnp.int32)) % count
    return jnp.take(stacked, order, axis=0)


def gather_up(shard):
    cols = shard.shape[1] // UP_DEPTH
    part = shard.reshape(cols, UP_DEPTH, BLK, BLK).transpose(0, 3, 1, 2)
    part = part.reshape(cols, BLK, UP_DEPTH * BLK)
    full = exchange_zh(part)
    full = lax.all_gather(full, ("y", "c"), axis=1, tiled=True)
    return full.reshape(-1, BLK, UP_DEPTH * BLK)


def gather_rows(shard):
    n = shard.shape[1]
    part = shard.reshape(n * 32, 128)
    full = exchange_zh(part)
    full = lax.all_gather(full, ("y", "c"), axis=1, tiled=True)
    return full.reshape(-1, 4096)


def make_layer(gain, up_index, up_values, down_index, down_values):
    width = gain.shape[0]
    hidden_width = up_values.shape[0] * BLK
    blocks_in = width // BLK
    blocks_hid = hidden_width // BLK
    weights_up = up_values
    weights_down = down_values.reshape(blocks_in, DOWN_DEPTH * BLK, BLK)
    gain_wide = gain.astype(jnp.float32)

    def layer(block):
        count = block.shape[0]
        wide = block.astype(jnp.float32)
        meansq = jnp.mean(wide * wide, axis=-1, keepdims=True)
        normed = (wide * lax.rsqrt(meansq + 1e-05) * gain_wide).astype(jnp.bfloat16)
        picked = normed.reshape(count, blocks_in, BLK)[:, up_index, :]
        picked = picked.reshape(count, blocks_hid, UP_DEPTH * BLK)
        up_sums = jnp.einsum("ncr,cjr->ncj", picked, weights_up, preferred_element_type=jnp.float32)
        hidden = jax.nn.gelu(up_sums, approximate=True).astype(jnp.bfloat16)
        second = hidden[:, down_index, :].reshape(count, blocks_in, DOWN_DEPTH * BLK)
        down_sums = jnp.einsum(
            "ncr,crj->ncj", second, weights_down, preferred_element_type=jnp.float32
        )
        return (wide + down_sums.reshape(count, width)).astype(jnp.bfloat16)

    return layer


def per_device(activations, keep, gains, up_rows, up_blocks, down_rows, down_blocks):
    up_all = gather_up(up_blocks)
    down_all = gather_rows(down_blocks)
    apply = make_layer(gains[0], up_rows[0].reshape(-1), up_all, down_rows[0].reshape(-1), down_all)
    places = jnp.cumsum(keep) - 1
    target = jnp.where(keep == 1, places, KEEP_DEV)
    chosen = (
        jnp.zeros((KEEP_DEV + 1,), jnp.int32)
        .at[target]
        .set(jnp.arange(keep.shape[0], dtype=jnp.int32))[:KEEP_DEV]
    )
    selected = activations[chosen]
    width = selected.shape[1]
    section = lax.axis_index(SEC)
    sections = lax.axis_size(SEC)
    pieces = 8
    group_rows = selected.shape[0] // pieces
    split = selected.reshape(pieces, group_rows, width)

    def advance(turn, held, record):
        offset = turn - section
        entry = jnp.where(section == 0, split[jnp.minimum(turn, pieces - 1)], held)
        active = (offset >= 0) & (offset < pieces)
        result = lax.cond(active, apply, jnp.zeros_like, entry)
        slot = jnp.clip(offset, 0, pieces - 1)
        current = lax.dynamic_index_in_dim(record, slot, 0, keepdims=False)
        updated = jnp.where(active, result, current)
        record = lax.dynamic_update_index_in_dim(record, updated, slot, 0)
        return (result, record)

    def turn_step(turn, carry):
        held, record = carry
        result, record = advance(turn, held, record)
        held = from_behind(result, SEC, 1)
        return (held, record)

    turns = sections + pieces - 1
    held, record = lax.fori_loop(0, turns, turn_step, (split[0], split))
    final = record.reshape(selected.shape[0], width)
    merged = activations.at[chosen].set(final)
    return merged[None]


def solution(mesh):
    zh = 4
    yc = mesh.shape["fsdp"] // zh
    zl = 2
    xs = mesh.shape["section"] // zl
    devices = mesh.devices.reshape(zl, xs, zh, yc // 2, 2)
    fine = Mesh(devices, ("zl", "x", "zh", "y", "c"))
    return jax.shard_map(
        per_device,
        mesh=fine,
        in_specs=(
            P(FS, None),
            P(FS),
            P(SEC, None),
            P(SEC, None, None),
            P(SEC, FS, None),
            P(SEC, None, None),
            P(SEC, FS, None),
        ),
        out_specs=P(SEC, FS, None),
        check_vma=False,
    )
```

profile of v0, /device:TPU:70, one launch (start us, length us, event | category | flops | bytes accessed | tf_op | source)
XLA Modules:
  0.0 516.3 jit_solution(16447429242946423552)
XLA Ops:
  8.2 6.1 %collective-permute-start.4 = (bf16[96,128]{1,0:T(8,128)(2,1)S(1)}, bf16[96,128]{1,0:T(8,128)(2,1)S(1)}, u32[]{:S(2)}, u32[]{:S(2)}) collective-permute-start(bf16[96,128]{1,0:T(8,128)(2,1)S(1)} %reshape.126), channel_id=1, source_target_pairs={{0,16},{16,32},{32,48},{48,0},{1,17},{17,33},{33,49},{49,1},{2,18}... | collective-permute-start | bytes 73736 | tf_op jit(solution)/shard_map/ppermute | solution.py:26
  14.3 8.2 %collective-permute-start.5 = (bf16[96,128]{1,0:T(8,128)(2,1)S(1)}, bf16[96,128]{1,0:T(8,128)(2,1)S(1)}, u32[]{:S(2)}, u32[]{:S(2)}) collective-permute-start(bf16[96,128]{1,0:T(8,128)(2,1)S(1)} %reshape.126), channel_id=1, source_target_pairs={{0,32},{16,48},{32,0},{48,16},{1,33},{17,49},{33,1},{49,17},{2,34}... | collective-permute-start | bytes 73736 | tf_op jit(solution)/shard_map/ppermute | solution.py:26
  22.5 3.7 collective-permute-start.6
  26.3 2.8 collective-permute-done.6
  30.9 3.1 collective-permute-start.1
  34.0 6.0 %collective-permute-start.2 = (bf16[3,64,128]{2,1,0:T(8,128)(2,1)S(1)}, bf16[3,64,128]{2,1,0:T(8,128)(2,1)S(1)}, u32[]{:S(2)}, u32[]{:S(2)}) collective-permute-start(bf16[3,64,128]{2,1,0:T(8,128)(2,1)S(1)} %reshape.124), channel_id=1, source_target_pairs={{0,32},{16,48},{32,0},{48,16},{1,33},{17,49},{33,1},{49,17},{2,34}... | collective-permute-start | bytes 147464 | tf_op jit(solution)/shard_map/ppermute | solution.py:26
  40.0 2.1 collective-permute-start.3
  42.2 2.1 collective-permute-done.2
  44.3 2.6 collective-permute-done.3
  50.1 2.6 gather_fusion.2
  53.7 2.8 copy.27
  57.7 12.9 %all-gather.5.cloned.1.call-done = bf16[4,1536,128]{2,1,0:T(8,128)(2,1)} async-done(((bf16[4,96,128]{2,1,0:T(8,128)(2,1)}), bf16[4,1536,128]{2,1,0:T(8,128)(2,1)}) %all-gather.5.cloned.1.call-update) | async-done | bytes 1572880 | tf_op jit(solution)/shard_map/all_gather | solution.py:45
  70.6 5.1 reshape_reshape.3
  75.7 4.3 copy.17
  80.0 34.8 %all-gather.3.cloned.1.call-done = bf16[4,48,64,128]{3,2,1,0:T(8,128)(2,1)} async-done(((bf16[4,3,64,128]{3,2,1,0:T(8,128)(2,1)}), bf16[4,48,64,128]{3,2,1,0:T(8,128)(2,1)}) %all-gather.3.cloned.1.call-update) | async-done | bytes 3145744 | tf_op jit(solution)/shard_map/all_gather | solution.py:37
  114.8 388.7 %while.16 = (s32[]{:T(128)}, bf16[16,6144]{1,0:T(8,128)(2,1)S(1)}, bf16[8,16,6144]{2,1,0:T(8,128)(2,1)}, s32[]{:T(128)}, pred[]{:T(512)}, /*index=5*/bf16[8,16,6...) while((s32[]{:T(128)}, bf16[16,6144]{1,0:T(8,128)(2,1)S(1)}, ...), condition=%wide.region_7.8_spmd, body=%wide.region_3.7_spmd.sunk | while | flops 78450392 | bytes 21276344 | solution.py:113
  117.8 5.9 %collective-permute-done = bf16[16,6144]{1,0:T(8,128)(2,1)S(1)} collective-permute-done((bf16[16,6144]{1,0:T(8,128)(2,1)S(1)}, bf16[16,6144]{1,0:T(8,128)(2,1)S(1)}, u32[]{:S(2)}, u32[]{:S(2)}) %collective-permute-start) | collective-permute-done | bytes 196640 | tf_op jit(solution)/shard_map/while/body/eval_jaxpr/ppermute | solution.py:18
  126.8 5.1 collective-permute-done
  134.9 4.6 collective-permute-done
  142.5 4.6 collective-permute-done
  150.1 4.7 collective-permute-done
  157.8 6.7 %collective-permute-done = bf16[16,6144]{1,0:T(8,128)(2,1)S(1)} collective-permute-done((bf16[16,6144]{1,0:T(8,128)(2,1)S(1)}, bf16[16,6144]{1,0:T(8,128)(2,1)S(1)}, u32[]{:S(2)}, u32[]{:S(2)}) %collective-permute-start) | collective-permute-done | bytes 196640 | tf_op jit(solution)/shard_map/while/body/eval_jaxpr/ppermute | solution.py:18
  167.5 119.1 %collective-permute-done = bf16[16,6144]{1,0:T(8,128)(2,1)S(1)} collective-permute-done((bf16[16,6144]{1,0:T(8,128)(2,1)S(1)}, bf16[16,6144]{1,0:T(8,128)(2,1)S(1)}, u32[]{:S(2)}, u32[]{:S(2)}) %collective-permute-start) | collective-permute-done | bytes 196640 | tf_op jit(solution)/shard_map/while/body/eval_jaxpr/ppermute | solution.py:18
  286.6 17.7 %conditional.2 = (bf16[16,6144]{1,0:T(8,128)(2,1)S(1)}) conditional(s32[]{:T(128)} %convert_element_type.52, () %tuple.47, (pred[]{:T(512)}, s32[]{:T(128)}, bf16[8,16,6144]{2,1,0:T(8,128)(2,1)}, bf16[16,6144]{1,0:T(8,128)(2,1)S(1)}, f32[6144]{0:T(1024)}, /*index=5*/s32[384]{0:T(512)S(1)}, bf16[192,64,128]{2,1,0:T(8,128)(2,1)}, s32[192]{0:T(256)S(1)}, ...), branch_computations={%region_4.4_spmd, %region_5.6_spmd} | conditional | flops 78352080 | bytes 19506548 | solution.py:99
  289.8 2.6 gather_fusion
  295.7 3.9 fusion.7
  301.0 2.3 convolution_bitcast_fusion
  307.3 6.7 %collective-permute-done = bf16[16,6144]{1,0:T(8,128)(2,1)S(1)} collective-permute-done((bf16[16,6144]{1,0:T(8,128)(2,1)S(1)}, bf16[16,6144]{1,0:T(8,128)(2,1)S(1)}, u32[]{:S(2)}, u32[]{:S(2)}) %collective-permute-start) | collective-permute-done | bytes 196640 | tf_op jit(solution)/shard_map/while/body/eval_jaxpr/ppermute | solution.py:18
  314.0 17.7 %conditional.2 = (bf16[16,6144]{1,0:T(8,128)(2,1)S(1)}) conditional(s32[]{:T(128)} %convert_element_type.52, () %tuple.47, (pred[]{:T(512)}, s32[]{:T(128)}, bf16[8,16,6144]{2,1,0:T(8,128)(2,1)}, bf16[16,6144]{1,0:T(8,128)(2,1)S(1)}, f32[6144]{0:T(1024)}, /*index=5*/s32[384]{0:T(512)S(1)}, bf16[192,64,128]{2,1,0:T(8,128)(2,1)}, s32[192]{0:T(256)S(1)}, ...), branch_computations={%region_4.4_spmd, %region_5.6_spmd} | conditional | flops 78352080 | bytes 19506548 | solution.py:99
  317.2 2.6 gather_fusion
  323.1 3.9 fusion.7
  328.3 2.3 convolution_bitcast_fusion
  334.7 6.7 %collective-permute-done = bf16[16,6144]{1,0:T(8,128)(2,1)S(1)} collective-permute-done((bf16[16,6144]{1,0:T(8,128)(2,1)S(1)}, bf16[16,6144]{1,0:T(8,128)(2,1)S(1)}, u32[]{:S(2)}, u32[]{:S(2)}) %collective-permute-start) | collective-permute-done | bytes 196640 | tf_op jit(solution)/shard_map/while/body/eval_jaxpr/ppermute | solution.py:18
  341.3 17.7 %conditional.2 = (bf16[16,6144]{1,0:T(8,128)(2,1)S(1)}) conditional(s32[]{:T(128)} %convert_element_type.52, () %tuple.47, (pred[]{:T(512)}, s32[]{:T(128)}, bf16[8,16,6144]{2,1,0:T(8,128)(2,1)}, bf16[16,6144]{1,0:T(8,128)(2,1)S(1)}, f32[6144]{0:T(1024)}, /*index=5*/s32[384]{0:T(512)S(1)}, bf16[192,64,128]{2,1,0:T(8,128)(2,1)}, s32[192]{0:T(256)S(1)}, ...), branch_computations={%region_4.4_spmd, %region_5.6_spmd} | conditional | flops 78352080 | bytes 19506548 | solution.py:99
  344.6 2.6 gather_fusion
  350.4 3.9 fusion.7
  355.7 2.3 convolution_bitcast_fusion
  362.0 6.7 %collective-permute-done = bf16[16,6144]{1,0:T(8,128)(2,1)S(1)} collective-permute-done((bf16[16,6144]{1,0:T(8,128)(2,1)S(1)}, bf16[16,6144]{1,0:T(8,128)(2,1)S(1)}, u32[]{:S(2)}, u32[]{:S(2)}) %collective-permute-start) | collective-permute-done | bytes 196640 | tf_op jit(solution)/shard_map/while/body/eval_jaxpr/ppermute | solution.py:18
  368.7 17.7 %conditional.2 = (bf16[16,6144]{1,0:T(8,128)(2,1)S(1)}) conditional(s32[]{:T(128)} %convert_element_type.52, () %tuple.47, (pred[]{:T(512)}, s32[]{:T(128)}, bf16[8,16,6144]{2,1,0:T(8,128)(2,1)}, bf16[16,6144]{1,0:T(8,128)(2,1)S(1)}, f32[6144]{0:T(1024)}, /*index=5*/s32[384]{0:T(512)S(1)}, bf16[192,64,128]{2,1,0:T(8,128)(2,1)}, s32[192]{0:T(256)S(1)}, ...), branch_computations={%region_4.4_spmd, %region_5.6_spmd} | conditional | flops 78352080 | bytes 19506548 | solution.py:99
  371.9 2.6 gather_fusion
  377.8 3.9 fusion.7
  383.1 2.3 convolution_bitcast_fusion
  389.4 6.7 %collective-permute-done = bf16[16,6144]{1,0:T(8,128)(2,1)S(1)} collective-permute-done((bf16[16,6144]{1,0:T(8,128)(2,1)S(1)}, bf16[16,6144]{1,0:T(8,128)(2,1)S(1)}, u32[]{:S(2)}, u32[]{:S(2)}) %collective-permute-start) | collective-permute-done | bytes 196640 | tf_op jit(solution)/shard_map/while/body/eval_jaxpr/ppermute | solution.py:18
  396.1 17.7 %conditional.2 = (bf16[16,6144]{1,0:T(8,128)(2,1)S(1)}) conditional(s32[]{:T(128)} %convert_element_type.52, () %tuple.47, (pred[]{:T(512)}, s32[]{:T(128)}, bf16[8,16,6144]{2,1,0:T(8,128)(2,1)}, bf16[16,6144]{1,0:T(8,128)(2,1)S(1)}, f32[6144]{0:T(1024)}, /*index=5*/s32[384]{0:T(512)S(1)}, bf16[192,64,128]{2,1,0:T(8,128)(2,1)}, s32[192]{0:T(256)S(1)}, ...), branch_computations={%region_4.4_spmd, %region_5.6_spmd} | conditional | flops 78352080 | bytes 19506548 | solution.py:99
  399.3 2.6 gather_fusion
  405.2 3.9 fusion.7
  410.5 2.3 convolution_bitcast_fusion
  416.8 6.7 %collective-permute-done = bf16[16,6144]{1,0:T(8,128)(2,1)S(1)} collective-permute-done((bf16[16,6144]{1,0:T(8,128)(2,1)S(1)}, bf16[16,6144]{1,0:T(8,128)(2,1)S(1)}, u32[]{:S(2)}, u32[]{:S(2)}) %collective-permute-start) | collective-permute-done | bytes 196640 | tf_op jit(solution)/shard_map/while/body/eval_jaxpr/ppermute | solution.py:18
  423.5 17.7 %conditional.2 = (bf16[16,6144]{1,0:T(8,128)(2,1)S(1)}) conditional(s32[]{:T(128)} %convert_element_type.52, () %tuple.47, (pred[]{:T(512)}, s32[]{:T(128)}, bf16[8,16,6144]{2,1,0:T(8,128)(2,1)}, bf16[16,6144]{1,0:T(8,128)(2,1)S(1)}, f32[6144]{0:T(1024)}, /*index=5*/s32[384]{0:T(512)S(1)}, bf16[192,64,128]{2,1,0:T(8,128)(2,1)}, s32[192]{0:T(256)S(1)}, ...), branch_computations={%region_4.4_spmd, %region_5.6_spmd} | conditional | flops 78352080 | bytes 19506548 | solution.py:99
  426.7 2.6 gather_fusion
  432.6 3.9 fusion.7
  437.8 2.3 convolution_bitcast_fusion
  444.2 6.7 %collective-permute-done = bf16[16,6144]{1,0:T(8,128)(2,1)S(1)} collective-permute-done((bf16[16,6144]{1,0:T(8,128)(2,1)S(1)}, bf16[16,6144]{1,0:T(8,128)(2,1)S(1)}, u32[]{:S(2)}, u32[]{:S(2)}) %collective-permute-start) | collective-permute-done | bytes 196640 | tf_op jit(solution)/shard_map/while/body/eval_jaxpr/ppermute | solution.py:18
  450.8 17.7 %conditional.2 = (bf16[16,6144]{1,0:T(8,128)(2,1)S(1)}) conditional(s32[]{:T(128)} %convert_element_type.52, () %tuple.47, (pred[]{:T(512)}, s32[]{:T(128)}, bf16[8,16,6144]{2,1,0:T(8,128)(2,1)}, bf16[16,6144]{1,0:T(8,128)(2,1)S(1)}, f32[6144]{0:T(1024)}, /*index=5*/s32[384]{0:T(512)S(1)}, bf16[192,64,128]{2,1,0:T(8,128)(2,1)}, s32[192]{0:T(256)S(1)}, ...), branch_computations={%region_4.4_spmd, %region_5.6_spmd} | conditional | flops 78352080 | bytes 19506548 | solution.py:99
  454.1 2.6 gather_fusion
  459.9 3.9 fusion.7
  465.2 2.3 convolution_bitcast_fusion
  471.5 6.7 %collective-permute-done = bf16[16,6144]{1,0:T(8,128)(2,1)S(1)} collective-permute-done((bf16[16,6144]{1,0:T(8,128)(2,1)S(1)}, bf16[16,6144]{1,0:T(8,128)(2,1)S(1)}, u32[]{:S(2)}, u32[]{:S(2)}) %collective-permute-start) | collective-permute-done | bytes 196640 | tf_op jit(solution)/shard_map/while/body/eval_jaxpr/ppermute | solution.py:18
  478.2 17.7 %conditional.2 = (bf16[16,6144]{1,0:T(8,128)(2,1)S(1)}) conditional(s32[]{:T(128)} %convert_element_type.52, () %tuple.47, (pred[]{:T(512)}, s32[]{:T(128)}, bf16[8,16,6144]{2,1,0:T(8,128)(2,1)}, bf16[16,6144]{1,0:T(8,128)(2,1)S(1)}, f32[6144]{0:T(1024)}, /*index=5*/s32[384]{0:T(512)S(1)}, bf16[192,64,128]{2,1,0:T(8,128)(2,1)}, s32[192]{0:T(256)S(1)}, ...), branch_computations={%region_4.4_spmd, %region_5.6_spmd} | conditional | flops 78352080 | bytes 19506548 | solution.py:99
  481.4 2.6 gather_fusion
  487.3 3.9 fusion.7
  492.6 2.3 convolution_bitcast_fusion
  498.9 4.6 collective-permute-done
  503.5 4.7 scatter_fusion
  (281 shorter events, 125.5 us)
Async XLA Ops:
  6.5 24.0 %copy-start.4 = (bf16[1,6,4096]{2,1,0:T(8,128)(2,1)S(1)}, bf16[1,6,4096]{2,1,0:T(8,128)(2,1)}, u32[]{:S(2)}) copy-start(bf16[1,6,4096]{2,1,0:T(8,128)(2,1)} %param.15) | copy-start | bytes 147460
  6.5 1.6 copy-start.3
  6.5 64.1 %all-gather.5.cloned.1.call-start = ((), (), s32[]{:S(2)}) async-start(), calls=%async_computation.1 | async-start | bytes 1671168 | tf_op jit(solution)/shard_map/all_gather | solution.py:45
  8.1 40.2 %copy-start.6 = (s32[160]{0:T(256)S(1)}, s32[160]{0:T(256)}, u32[]{:S(2)}) copy-start(s32[160]{0:T(256)} %param.12) | copy-start | bytes 1924
  8.2 18.1 %collective-permute-start.4 = (bf16[96,128]{1,0:T(8,128)(2,1)S(1)}, bf16[96,128]{1,0:T(8,128)(2,1)S(1)}, u32[]{:S(2)}, u32[]{:S(2)}) collective-permute-start(bf16[96,128]{1,0:T(8,128)(2,1)S(1)} %reshape.126), channel_id=1, source_target_pairs={{0,16},{16,32},{32,48},{48,0},{1,17},{17,33},{33,49},{49,1},{2,18}... | collective-permute-start | bytes 73736 | tf_op jit(solution)/shard_map/ppermute | solution.py:26
  14.3 12.0 %collective-permute-start.5 = (bf16[96,128]{1,0:T(8,128)(2,1)S(1)}, bf16[96,128]{1,0:T(8,128)(2,1)S(1)}, u32[]{:S(2)}, u32[]{:S(2)}) collective-permute-start(bf16[96,128]{1,0:T(8,128)(2,1)S(1)} %reshape.126), channel_id=1, source_target_pairs={{0,32},{16,48},{32,0},{48,16},{1,33},{17,49},{33,1},{49,17},{2,34}... | collective-permute-start | bytes 73736 | tf_op jit(solution)/shard_map/ppermute | solution.py:26
  22.5 6.6 %collective-permute-start.6 = (bf16[96,128]{1,0:T(8,128)(2,1)S(1)}, bf16[96,128]{1,0:T(8,128)(2,1)S(1)}, u32[]{:S(2)}, u32[]{:S(2)}) collective-permute-start(bf16[96,128]{1,0:T(8,128)(2,1)S(1)} %reshape.126), channel_id=1, source_target_pairs={{0,48},{16,0},{32,16},{48,32},{1,49},{17,1},{33,17},{49,33},{2,50}... | collective-permute-start | bytes 73736 | tf_op jit(solution)/shard_map/ppermute | solution.py:26
  30.5 84.3 %all-gather.3.cloned.1.call-start = ((), (), s32[]{:S(2)}) async-start(), calls=%async_computation | async-start | bytes 3342336 | tf_op jit(solution)/shard_map/all_gather | solution.py:37
  30.9 11.3 %collective-permute-start.1 = (bf16[3,64,128]{2,1,0:T(8,128)(2,1)S(1)}, bf16[3,64,128]{2,1,0:T(8,128)(2,1)S(1)}, u32[]{:S(2)}, u32[]{:S(2)}) collective-permute-start(bf16[3,64,128]{2,1,0:T(8,128)(2,1)S(1)} %reshape.124), channel_id=1, source_target_pairs={{0,16},{16,32},{32,48},{48,0},{1,17},{17,33},{33,49},{49,1},{2,18}... | collective-permute-start | bytes 147464 | tf_op jit(solution)/shard_map/ppermute | solution.py:26
  34.0 10.3 %collective-permute-start.2 = (bf16[3,64,128]{2,1,0:T(8,128)(2,1)S(1)}, bf16[3,64,128]{2,1,0:T(8,128)(2,1)S(1)}, u32[]{:S(2)}, u32[]{:S(2)}) collective-permute-start(bf16[3,64,128]{2,1,0:T(8,128)(2,1)S(1)} %reshape.124), channel_id=1, source_target_pairs={{0,32},{16,48},{32,0},{48,16},{1,33},{17,49},{33,1},{49,17},{2,34}... | collective-permute-start | bytes 147464 | tf_op jit(solution)/shard_map/ppermute | solution.py:26
  40.0 6.9 %collective-permute-start.3 = (bf16[3,64,128]{2,1,0:T(8,128)(2,1)S(1)}, bf16[3,64,128]{2,1,0:T(8,128)(2,1)S(1)}, u32[]{:S(2)}, u32[]{:S(2)}) collective-permute-start(bf16[3,64,128]{2,1,0:T(8,128)(2,1)S(1)} %reshape.124), channel_id=1, source_target_pairs={{0,48},{16,0},{32,16},{48,32},{1,49},{17,1},{33,17},{49,33},{2,50}... | collective-permute-start | bytes 147464 | tf_op jit(solution)/shard_map/ppermute | solution.py:26
  53.7 2.8 copy-start.7
  53.7 3.1 copy-start.8
  53.7 3.3 copy-start.5
  114.9 8.9 %collective-permute-start = (bf16[16,6144]{1,0:T(8,128)(2,1)S(1)}, bf16[16,6144]{1,0:T(8,128)(2,1)S(1)}, u32[]{:S(2)}, u32[]{:S(2)}) collective-permute-start(bf16[16,6144]{1,0:T(8,128)(2,1)S(1)} %get-tuple-element.467), channel_id=1, source_target_pairs={{0,64},{64,128},{128,192},{192,256},{256,320},{320,384},{384,448},... | collective-permute-start | bytes 589832 | tf_op jit(solution)/shard_map/while/body/eval_jaxpr/ppermute | solution.py:18
  123.8 8.1 %collective-permute-start = (bf16[16,6144]{1,0:T(8,128)(2,1)S(1)}, bf16[16,6144]{1,0:T(8,128)(2,1)S(1)}, u32[]{:S(2)}, u32[]{:S(2)}) collective-permute-start(bf16[16,6144]{1,0:T(8,128)(2,1)S(1)} %get-tuple-element.467), channel_id=1, source_target_pairs={{0,64},{64,128},{128,192},{192,256},{256,320},{320,384},{384,448},... | collective-permute-start | bytes 589832 | tf_op jit(solution)/shard_map/while/body/eval_jaxpr/ppermute | solution.py:18
  131.9 7.6 %collective-permute-start = (bf16[16,6144]{1,0:T(8,128)(2,1)S(1)}, bf16[16,6144]{1,0:T(8,128)(2,1)S(1)}, u32[]{:S(2)}, u32[]{:S(2)}) collective-permute-start(bf16[16,6144]{1,0:T(8,128)(2,1)S(1)} %get-tuple-element.467), channel_id=1, source_target_pairs={{0,64},{64,128},{128,192},{192,256},{256,320},{320,384},{384,448},... | collective-permute-start | bytes 589832 | tf_op jit(solution)/shard_map/while/body/eval_jaxpr/ppermute | solution.py:18
  139.5 7.6 %collective-permute-start = (bf16[16,6144]{1,0:T(8,128)(2,1)S(1)}, bf16[16,6144]{1,0:T(8,128)(2,1)S(1)}, u32[]{:S(2)}, u32[]{:S(2)}) collective-permute-start(bf16[16,6144]{1,0:T(8,128)(2,1)S(1)} %get-tuple-element.467), channel_id=1, source_target_pairs={{0,64},{64,128},{128,192},{192,256},{256,320},{320,384},{384,448},... | collective-permute-start | bytes 589832 | tf_op jit(solution)/shard_map/while/body/eval_jaxpr/ppermute | solution.py:18
  147.1 7.7 %collective-permute-start = (bf16[16,6144]{1,0:T(8,128)(2,1)S(1)}, bf16[16,6144]{1,0:T(8,128)(2,1)S(1)}, u32[]{:S(2)}, u32[]{:S(2)}) collective-permute-start(bf16[16,6144]{1,0:T(8,128)(2,1)S(1)} %get-tuple-element.467), channel_id=1, source_target_pairs={{0,64},{64,128},{128,192},{192,256},{256,320},{320,384},{384,448},... | collective-permute-start | bytes 589832 | tf_op jit(solution)/shard_map/while/body/eval_jaxpr/ppermute | solution.py:18
  154.8 9.7 %collective-permute-start = (bf16[16,6144]{1,0:T(8,128)(2,1)S(1)}, bf16[16,6144]{1,0:T(8,128)(2,1)S(1)}, u32[]{:S(2)}, u32[]{:S(2)}) collective-permute-start(bf16[16,6144]{1,0:T(8,128)(2,1)S(1)} %get-tuple-element.467), channel_id=1, source_target_pairs={{0,64},{64,128},{128,192},{192,256},{256,320},{320,384},{384,448},... | collective-permute-start | bytes 589832 | tf_op jit(solution)/shard_map/while/body/eval_jaxpr/ppermute | solution.py:18
  164.5 122.1 %collective-permute-start = (bf16[16,6144]{1,0:T(8,128)(2,1)S(1)}, bf16[16,6144]{1,0:T(8,128)(2,1)S(1)}, u32[]{:S(2)}, u32[]{:S(2)}) collective-permute-start(bf16[16,6144]{1,0:T(8,128)(2,1)S(1)} %get-tuple-element.467), channel_id=1, source_target_pairs={{0,64},{64,128},{128,192},{192,256},{256,320},{320,384},{384,448},... | collective-permute-start | bytes 589832 | tf_op jit(solution)/shard_map/while/body/eval_jaxpr/ppermute | solution.py:18
  287.7 0.7 copy-start.1
  303.3 0.9 copy-start.2
  304.3 9.7 %collective-permute-start = (bf16[16,6144]{1,0:T(8,128)(2,1)S(1)}, bf16[16,6144]{1,0:T(8,128)(2,1)S(1)}, u32[]{:S(2)}, u32[]{:S(2)}) collective-permute-start(bf16[16,6144]{1,0:T(8,128)(2,1)S(1)} %get-tuple-element.467), channel_id=1, source_target_pairs={{0,64},{64,128},{128,192},{192,256},{256,320},{320,384},{384,448},... | collective-permute-start | bytes 589832 | tf_op jit(solution)/shard_map/while/body/eval_jaxpr/ppermute | solution.py:18
  315.1 0.7 copy-start.1
  330.7 0.9 copy-start.2
  331.7 9.7 %collective-permute-start = (bf16[16,6144]{1,0:T(8,128)(2,1)S(1)}, bf16[16,6144]{1,0:T(8,128)(2,1)S(1)}, u32[]{:S(2)}, u32[]{:S(2)}) collective-permute-start(bf16[16,6144]{1,0:T(8,128)(2,1)S(1)} %get-tuple-element.467), channel_id=1, source_target_pairs={{0,64},{64,128},{128,192},{192,256},{256,320},{320,384},{384,448},... | collective-permute-start | bytes 589832 | tf_op jit(solution)/shard_map/while/body/eval_jaxpr/ppermute | solution.py:18
  342.4 0.7 copy-start.1
  358.0 0.9 copy-start.2
  359.0 9.7 %collective-permute-start = (bf16[16,6144]{1,0:T(8,128)(2,1)S(1)}, bf16[16,6144]{1,0:T(8,128)(2,1)S(1)}, u32[]{:S(2)}, u32[]{:S(2)}) collective-permute-start(bf16[16,6144]{1,0:T(8,128)(2,1)S(1)} %get-tuple-element.467), channel_id=1, source_target_pairs={{0,64},{64,128},{128,192},{192,256},{256,320},{320,384},{384,448},... | collective-permute-start | bytes 589832 | tf_op jit(solution)/shard_map/while/body/eval_jaxpr/ppermute | solution.py:18
  369.8 0.7 copy-start.1
  385.4 0.9 copy-start.2
  386.4 9.7 %collective-permute-start = (bf16[16,6144]{1,0:T(8,128)(2,1)S(1)}, bf16[16,6144]{1,0:T(8,128)(2,1)S(1)}, u32[]{:S(2)}, u32[]{:S(2)}) collective-permute-start(bf16[16,6144]{1,0:T(8,128)(2,1)S(1)} %get-tuple-element.467), channel_id=1, source_target_pairs={{0,64},{64,128},{128,192},{192,256},{256,320},{320,384},{384,448},... | collective-permute-start | bytes 589832 | tf_op jit(solution)/shard_map/while/body/eval_jaxpr/ppermute | solution.py:18
  397.2 0.7 copy-start.1
  412.8 0.9 copy-start.2
  413.8 9.7 %collective-permute-start = (bf16[16,6144]{1,0:T(8,128)(2,1)S(1)}, bf16[16,6144]{1,0:T(8,128)(2,1)S(1)}, u32[]{:S(2)}, u32[]{:S(2)}) collective-permute-start(bf16[16,6144]{1,0:T(8,128)(2,1)S(1)} %get-tuple-element.467), channel_id=1, source_target_pairs={{0,64},{64,128},{128,192},{192,256},{256,320},{320,384},{384,448},... | collective-permute-start | bytes 589832 | tf_op jit(solution)/shard_map/while/body/eval_jaxpr/ppermute | solution.py:18
  424.6 0.7 copy-start.1
  440.2 0.9 copy-start.2
  441.2 9.7 %collective-permute-start = (bf16[16,6144]{1,0:T(8,128)(2,1)S(1)}, bf16[16,6144]{1,0:T(8,128)(2,1)S(1)}, u32[]{:S(2)}, u32[]{:S(2)}) collective-permute-start(bf16[16,6144]{1,0:T(8,128)(2,1)S(1)} %get-tuple-element.467), channel_id=1, source_target_pairs={{0,64},{64,128},{128,192},{192,256},{256,320},{320,384},{384,448},... | collective-permute-start | bytes 589832 | tf_op jit(solution)/shard_map/while/body/eval_jaxpr/ppermute | solution.py:18
  451.9 0.7 copy-start.1
  467.5 0.9 copy-start.2
  468.5 9.7 %collective-permute-start = (bf16[16,6144]{1,0:T(8,128)(2,1)S(1)}, bf16[16,6144]{1,0:T(8,128)(2,1)S(1)}, u32[]{:S(2)}, u32[]{:S(2)}) collective-permute-start(bf16[16,6144]{1,0:T(8,128)(2,1)S(1)} %get-tuple-element.467), channel_id=1, source_target_pairs={{0,64},{64,128},{128,192},{192,256},{256,320},{320,384},{384,448},... | collective-permute-start | bytes 589832 | tf_op jit(solution)/shard_map/while/body/eval_jaxpr/ppermute | solution.py:18
  479.3 0.7 copy-start.1
  494.9 0.9 copy-start.2
  495.9 7.6 %collective-permute-start = (bf16[16,6144]{1,0:T(8,128)(2,1)S(1)}, bf16[16,6144]{1,0:T(8,128)(2,1)S(1)}, u32[]{:S(2)}, u32[]{:S(2)}) collective-permute-start(bf16[16,6144]{1,0:T(8,128)(2,1)S(1)} %get-tuple-element.467), channel_id=1, source_target_pairs={{0,64},{64,128},{128,192},{192,256},{256,320},{320,384},{384,448},... | collective-permute-start | bytes 589832 | tf_op jit(solution)/shard_map/while/body/eval_jaxpr/ppermute | solution.py:18
  508.2 1.3 copy-start
Sparse Core Ops, SparseCore 0:
  30.6 39.9 all-gather.4
  72.7 42.0 all-gather.2
where the time goes:
time: 519 us; the launch traced here: 516 us
  waiting for transfers between devices  257 us (50%)
  local copies, waits for them, and re-layouts  116 us (22%)
  matrix products  49.8 us (10%)
  starting transfers between devices  48.6 us (9%)
  other arithmetic  29.9 us (6%)
  between operations  13.7 us (3%)
    ppermute x15, waiting for transfers between devices, from_behind(): lax.ppermute(value, axis, [(source, source + steps) for source in range(i...  202 us
    gather x16, local copies, waits for them, and re-layouts, layer(): picked = normed.reshape(count, blocks_in, BLK)[:, up_index, :]  35 us
    all_gather x1, waiting for transfers between devices, gather_up(): full = lax.all_gather(full, ('y', 'c'), axis=1, tiled=True)  34.8 us
    dot_general x8, matrix products, layer(): jnp.einsum('ncr,cjr->ncj', picked, weights_up, preferred_element_type=jnp...  31.2 us
    ppermute x6, starting transfers between devices, exchange_zh(): lax.ppermute(part, 'zh', [(i, (i + shift) % count) for i in range(count)])  29.2 us
    ppermute x15, starting transfers between devices, from_behind(): lax.ppermute(value, axis, [(source, source + steps) for source in range(i...  19.4 us
    dot_general x8, matrix products, layer(): jnp.einsum('ncr,crj->ncj', second, weights_down, preferred_element_type=j...  18.6 us
    dynamic_slice x15, local copies, waits for them, and re-layouts, advance(): current = lax.dynamic_index_in_dim(record, slot, 0, keepdims=False)  14.2 us
  transfers between devices with their start and end apart: 23, of which 20 were waited for; matrix products, arithmetic and copies ran while one was open for 9% of the time, Pallas kernels for 0%

commit v1 on v0

--- a/solution.py
+++ b/solution.py
@@ -10,6 +10,15 @@
 KEEP_DEV = 128
 SEC = ("zl", "x")
 FS = ("zh", "y", "c")
+
+
+def settle_map(base_x):
+    arr_out = jax.lax.psum(1, ("y", "c"))
+    g_now = jnp.stack(arr_out * [base_x], axis=0)
+    near = jnp.concatenate(
+        jax.lax.all_to_all(g_now, ("y", "c"), split_axis=0, concat_axis=0), axis=1
+    )
+    return near
 
 
 def from_behind(value, axis, steps):
@@ -42,7 +51,7 @@
     n = shard.shape[1]
     part = shard.reshape(n * 32, 128)
     full = exchange_zh(part)
-    full = lax.all_gather(full, ("y", "c"), axis=1, tiled=True)
+    full = settle_map(full)
     return full.reshape(-1, 4096)
 
 

time: 519 us -> 515 us (level)
  waiting for transfers between devices: 257 us -> 242 us
  starting transfers between devices: 48.6 us -> 56.4 us
    all_gather x1, waiting for transfers between devices: 34.8 us -> 0.01 us  [gather_up(): full = lax.all_gather(full, ('y', 'c'), axis=1, tiled=True)]
    all_to_all x0 -> x1, waiting for transfers between devices: none -> 34 us  [settle_map(): jax.lax.all_to_all(g_now, ('y', 'c'), split_axis=0, concat_axis=0)]
    all_gather x1 -> x0, waiting for transfers between devices: 12.9 us -> none  [gather_rows(): full = lax.all_gather(full, ('y', 'c'), axis=1, tiled=True)]
    all_to_all x0 -> x1, starting transfers between devices: none -> 7.38 us  [settle_map(): jax.lax.all_to_all(g_now, ('y', 'c'), split_axis=0, concat_axis=0)]
  transfers between devices with their start and end apart: 23 -> 23, of which waited for: 20 -> 19; matrix products, arithmetic and copies ran while one was open for 9% -> 10% of each run, Pallas kernels for 0% -> 0%
where the time goes in v1:
time: 515 us; the launch traced here: 513 us
  waiting for transfers between devices  242 us (47%)
  local copies, waits for them, and re-layouts  120 us (23%)
  starting transfers between devices  56.4 us (11%)
  matrix products  49.8 us (10%)
  other arithmetic  29.2 us (6%)
  between operations  13.7 us (3%)
    ppermute x15, waiting for transfers between devices, from_behind(): lax.ppermute(value, axis, [(source, source + steps) for source in range(i...  201 us
    gather x16, local copies, waits for them, and re-layouts, layer(): picked = normed.reshape(count, blocks_in, BLK)[:, up_index, :]  35 us
    all_to_all x1, waiting for transfers between devices, settle_map(): jax.lax.all_to_all(g_now, ('y', 'c'), split_axis=0, concat_axis=0)  34 us
    dot_general x8, matrix products, layer(): jnp.einsum('ncr,cjr->ncj', picked, weights_up, preferred_element_type=jnp...  31.2 us
    ppermute x6, starting transfers between devices, exchange_zh(): lax.ppermute(part, 'zh', [(i, (i + shift) % count) for i in range(count)])  29.6 us
    ppermute x15, starting transfers between devices, from_behind(): lax.ppermute(value, axis, [(source, source + steps) for source in range(i...  19.4 us
    dot_general x8, matrix products, layer(): jnp.einsum('ncr,crj->ncj', second, weights_down, preferred_element_type=j...  18.6 us
    dynamic_slice x15, local copies, waits for them, and re-layouts, advance(): current = lax.dynamic_index_in_dim(record, slot, 0, keepdims=False)  14.2 us
  transfers between devices with their start and end apart: 23, of which 19 were waited for; matrix products, arithmetic and copies ran while one was open for 10% of the time, Pallas kernels for 0%

profile of v1, /device:TPU:70, one launch (start us, length us, event | category | flops | bytes accessed | tf_op | source)
XLA Modules:
  0.0 512.5 jit_solution(11915193510586564001)
XLA Ops:
  8.5 6.1 %collective-permute-start.1 = (bf16[3,64,128]{2,1,0:T(8,128)(2,1)S(1)}, bf16[3,64,128]{2,1,0:T(8,128)(2,1)S(1)}, u32[]{:S(2)}, u32[]{:S(2)}) collective-permute-start(bf16[3,64,128]{2,1,0:T(8,128)(2,1)S(1)} %reshape.129), channel_id=1, source_target_pairs={{0,16},{16,32},{32,48},{48,0},{1,17},{17,33},{33,49},{49,1},{2,18}... | collective-permute-start | bytes 147464 | tf_op jit(solution)/shard_map/ppermute | solution.py:35
  14.6 8.2 %collective-permute-start.2 = (bf16[3,64,128]{2,1,0:T(8,128)(2,1)S(1)}, bf16[3,64,128]{2,1,0:T(8,128)(2,1)S(1)}, u32[]{:S(2)}, u32[]{:S(2)}) collective-permute-start(bf16[3,64,128]{2,1,0:T(8,128)(2,1)S(1)} %reshape.129), channel_id=1, source_target_pairs={{0,32},{16,48},{32,0},{48,16},{1,33},{17,49},{33,1},{49,17},{2,34}... | collective-permute-start | bytes 147464 | tf_op jit(solution)/shard_map/ppermute | solution.py:35
  22.8 3.7 collective-permute-start.3
  26.7 3.5 collective-permute-done.3
  31.6 2.7 collective-permute-start.4
  34.3 6.5 %collective-permute-start.5 = (bf16[96,128]{1,0:T(8,128)(2,1)S(1)}, bf16[96,128]{1,0:T(8,128)(2,1)S(1)}, u32[]{:S(2)}, u32[]{:S(2)}) collective-permute-start(bf16[96,128]{1,0:T(8,128)(2,1)S(1)} %reshape.131), channel_id=1, source_target_pairs={{0,32},{16,48},{32,0},{48,16},{1,33},{17,49},{33,1},{49,17},{2,34}... | collective-permute-start | bytes 73736 | tf_op jit(solution)/shard_map/ppermute | solution.py:35
  40.8 2.5 collective-permute-start.6
  44.0 3.4 collective-permute-done.6
  49.5 7.4 %all-to-all-start = ((bf16[16,4,96,128]{3,2,1,0:T(8,128)(2,1)}), bf16[16,4,96,128]{3,2,1,0:T(8,128)(2,1)}, u32[]{:S(2)}, u32[]{:S(2)}) async-start(bf16[16,4,96,128]{3,2,1,0:T(8,128)(2,1)} %stack.51), calls=%async_computation | async-start | bytes 3145728 | tf_op jit(solution)/shard_map/all_to_all | solution.py:19
  58.7 2.6 gather_fusion.2
  62.3 2.8 copy.38
  66.3 34.0 %all-to-all-done = bf16[16,4,96,128]{3,2,1,0:T(8,128)(2,1)} async-done(((bf16[16,4,96,128]{3,2,1,0:T(8,128)(2,1)}), bf16[16,4,96,128]{3,2,1,0:T(8,128)(2,1)}, u32[]{:S(2)}, u32[]{:S(2)}) %all-to-all-start) | async-done | bytes 1572896 | tf_op jit(solution)/shard_map/all_to_all | solution.py:19
  100.3 2.7 copy.27
  103.0 5.1 reshape_reshape_reshape.3
  108.1 4.3 copy.28
  112.3 387.4 %while.16 = (s32[]{:T(128)}, bf16[16,6144]{1,0:T(8,128)(2,1)S(1)}, bf16[8,16,6144]{2,1,0:T(8,128)(2,1)}, s32[]{:T(128)}, pred[]{:T(512)}, /*index=5*/bf16[8,16,6...) while((s32[]{:T(128)}, bf16[16,6144]{1,0:T(8,128)(2,1)S(1)}, ...), condition=%wide.region_7.8_spmd, body=%wide.region_3.7_spmd.sunk | while | flops 78450392 | bytes 21276344 | solution.py:122
  115.4 5.6 %collective-permute-done = bf16[16,6144]{1,0:T(8,128)(2,1)S(1)} collective-permute-done((bf16[16,6144]{1,0:T(8,128)(2,1)S(1)}, bf16[16,6144]{1,0:T(8,128)(2,1)S(1)}, u32[]{:S(2)}, u32[]{:S(2)}) %collective-permute-start) | collective-permute-done | bytes 196640 | tf_op jit(solution)/shard_map/while/body/eval_jaxpr/ppermute | solution.py:27
  124.0 4.8 collective-permute-done
  131.8 4.6 collective-permute-done
  139.4 4.6 collective-permute-done
  147.0 4.8 collective-permute-done
  154.7 6.7 %collective-permute-done = bf16[16,6144]{1,0:T(8,128)(2,1)S(1)} collective-permute-done((bf16[16,6144]{1,0:T(8,128)(2,1)S(1)}, bf16[16,6144]{1,0:T(8,128)(2,1)S(1)}, u32[]{:S(2)}, u32[]{:S(2)}) %collective-permute-start) | collective-permute-done | bytes 196640 | tf_op jit(solution)/shard_map/while/body/eval_jaxpr/ppermute | solution.py:27
  164.4 118.6 %collective-permute-done = bf16[16,6144]{1,0:T(8,128)(2,1)S(1)} collective-permute-done((bf16[16,6144]{1,0:T(8,128)(2,1)S(1)}, bf16[16,6144]{1,0:T(8,128)(2,1)S(1)}, u32[]{:S(2)}, u32[]{:S(2)}) %collective-permute-start) | collective-permute-done | bytes 196640 | tf_op jit(solution)/shard_map/while/body/eval_jaxpr/ppermute | solution.py:27
  283.0 17.7 %conditional.2 = (bf16[16,6144]{1,0:T(8,128)(2,1)S(1)}) conditional(s32[]{:T(128)} %convert_element_type.52, () %tuple.48, (pred[]{:T(512)}, s32[]{:T(128)}, bf16[8,16,6144]{2,1,0:T(8,128)(2,1)}, bf16[16,6144]{1,0:T(8,128)(2,1)S(1)}, f32[6144]{0:T(1024)}, /*index=5*/s32[384]{0:T(512)S(1)}, bf16[192,64,128]{2,1,0:T(8,128)(2,1)}, s32[192]{0:T(256)S(1)}, ...), branch_computations={%region_4.4_spmd, %region_5.6_spmd} | conditional | flops 78352080 | bytes 19506548 | solution.py:108
  286.3 2.6 gather_fusion
  292.1 3.9 fusion.7
  297.4 2.3 convolution_bitcast_fusion
  303.7 6.7 %collective-permute-done = bf16[16,6144]{1,0:T(8,128)(2,1)S(1)} collective-permute-done((bf16[16,6144]{1,0:T(8,128)(2,1)S(1)}, bf16[16,6144]{1,0:T(8,128)(2,1)S(1)}, u32[]{:S(2)}, u32[]{:S(2)}) %collective-permute-start) | collective-permute-done | bytes 196640 | tf_op jit(solution)/shard_map/while/body/eval_jaxpr/ppermute | solution.py:27
  310.4 17.7 %conditional.2 = (bf16[16,6144]{1,0:T(8,128)(2,1)S(1)}) conditional(s32[]{:T(128)} %convert_element_type.52, () %tuple.48, (pred[]{:T(512)}, s32[]{:T(128)}, bf16[8,16,6144]{2,1,0:T(8,128)(2,1)}, bf16[16,6144]{1,0:T(8,128)(2,1)S(1)}, f32[6144]{0:T(1024)}, /*index=5*/s32[384]{0:T(512)S(1)}, bf16[192,64,128]{2,1,0:T(8,128)(2,1)}, s32[192]{0:T(256)S(1)}, ...), branch_computations={%region_4.4_spmd, %region_5.6_spmd} | conditional | flops 78352080 | bytes 19506548 | solution.py:108
  313.6 2.6 gather_fusion
  319.5 3.9 fusion.7
  324.7 2.3 convolution_bitcast_fusion
  331.1 6.7 %collective-permute-done = bf16[16,6144]{1,0:T(8,128)(2,1)S(1)} collective-permute-done((bf16[16,6144]{1,0:T(8,128)(2,1)S(1)}, bf16[16,6144]{1,0:T(8,128)(2,1)S(1)}, u32[]{:S(2)}, u32[]{:S(2)}) %collective-permute-start) | collective-permute-done | bytes 196640 | tf_op jit(solution)/shard_map/while/body/eval_jaxpr/ppermute | solution.py:27
  337.7 17.7 %conditional.2 = (bf16[16,6144]{1,0:T(8,128)(2,1)S(1)}) conditional(s32[]{:T(128)} %convert_element_type.52, () %tuple.48, (pred[]{:T(512)}, s32[]{:T(128)}, bf16[8,16,6144]{2,1,0:T(8,128)(2,1)}, bf16[16,6144]{1,0:T(8,128)(2,1)S(1)}, f32[6144]{0:T(1024)}, /*index=5*/s32[384]{0:T(512)S(1)}, bf16[192,64,128]{2,1,0:T(8,128)(2,1)}, s32[192]{0:T(256)S(1)}, ...), branch_computations={%region_4.4_spmd, %region_5.6_spmd} | conditional | flops 78352080 | bytes 19506548 | solution.py:108
  340.9 2.6 gather_fusion
  346.8 3.9 fusion.7
  352.1 2.3 convolution_bitcast_fusion
  358.4 6.7 %collective-permute-done = bf16[16,6144]{1,0:T(8,128)(2,1)S(1)} collective-permute-done((bf16[16,6144]{1,0:T(8,128)(2,1)S(1)}, bf16[16,6144]{1,0:T(8,128)(2,1)S(1)}, u32[]{:S(2)}, u32[]{:S(2)}) %collective-permute-start) | collective-permute-done | bytes 196640 | tf_op jit(solution)/shard_map/while/body/eval_jaxpr/ppermute | solution.py:27
  365.1 17.7 %conditional.2 = (bf16[16,6144]{1,0:T(8,128)(2,1)S(1)}) conditional(s32[]{:T(128)} %convert_element_type.52, () %tuple.48, (pred[]{:T(512)}, s32[]{:T(128)}, bf16[8,16,6144]{2,1,0:T(8,128)(2,1)}, bf16[16,6144]{1,0:T(8,128)(2,1)S(1)}, f32[6144]{0:T(1024)}, /*index=5*/s32[384]{0:T(512)S(1)}, bf16[192,64,128]{2,1,0:T(8,128)(2,1)}, s32[192]{0:T(256)S(1)}, ...), branch_computations={%region_4.4_spmd, %region_5.6_spmd} | conditional | flops 78352080 | bytes 19506548 | solution.py:108
  368.3 2.6 gather_fusion
  374.2 3.9 fusion.7
  379.4 2.3 convolution_bitcast_fusion
  385.8 6.7 %collective-permute-done = bf16[16,6144]{1,0:T(8,128)(2,1)S(1)} collective-permute-done((bf16[16,6144]{1,0:T(8,128)(2,1)S(1)}, bf16[16,6144]{1,0:T(8,128)(2,1)S(1)}, u32[]{:S(2)}, u32[]{:S(2)}) %collective-permute-start) | collective-permute-done | bytes 196640 | tf_op jit(solution)/shard_map/while/body/eval_jaxpr/ppermute | solution.py:27
  392.4 17.7 %conditional.2 = (bf16[16,6144]{1,0:T(8,128)(2,1)S(1)}) conditional(s32[]{:T(128)} %convert_element_type.52, () %tuple.48, (pred[]{:T(512)}, s32[]{:T(128)}, bf16[8,16,6144]{2,1,0:T(8,128)(2,1)}, bf16[16,6144]{1,0:T(8,128)(2,1)S(1)}, f32[6144]{0:T(1024)}, /*index=5*/s32[384]{0:T(512)S(1)}, bf16[192,64,128]{2,1,0:T(8,128)(2,1)}, s32[192]{0:T(256)S(1)}, ...), branch_computations={%region_4.4_spmd, %region_5.6_spmd} | conditional | flops 78352080 | bytes 19506548 | solution.py:108
  395.6 2.6 gather_fusion
  401.5 3.9 fusion.7
  406.8 2.3 convolution_bitcast_fusion
  413.1 6.7 %collective-permute-done = bf16[16,6144]{1,0:T(8,128)(2,1)S(1)} collective-permute-done((bf16[16,6144]{1,0:T(8,128)(2,1)S(1)}, bf16[16,6144]{1,0:T(8,128)(2,1)S(1)}, u32[]{:S(2)}, u32[]{:S(2)}) %collective-permute-start) | collective-permute-done | bytes 196640 | tf_op jit(solution)/shard_map/while/body/eval_jaxpr/ppermute | solution.py:27
  419.8 17.7 %conditional.2 = (bf16[16,6144]{1,0:T(8,128)(2,1)S(1)}) conditional(s32[]{:T(128)} %convert_element_type.52, () %tuple.48, (pred[]{:T(512)}, s32[]{:T(128)}, bf16[8,16,6144]{2,1,0:T(8,128)(2,1)}, bf16[16,6144]{1,0:T(8,128)(2,1)S(1)}, f32[6144]{0:T(1024)}, /*index=5*/s32[384]{0:T(512)S(1)}, bf16[192,64,128]{2,1,0:T(8,128)(2,1)}, s32[192]{0:T(256)S(1)}, ...), branch_computations={%region_4.4_spmd, %region_5.6_spmd} | conditional | flops 78352080 | bytes 19506548 | solution.py:108
  423.0 2.6 gather_fusion
  428.9 3.9 fusion.7
  434.1 2.3 convolution_bitcast_fusion
  440.4 6.7 %collective-permute-done = bf16[16,6144]{1,0:T(8,128)(2,1)S(1)} collective-permute-done((bf16[16,6144]{1,0:T(8,128)(2,1)S(1)}, bf16[16,6144]{1,0:T(8,128)(2,1)S(1)}, u32[]{:S(2)}, u32[]{:S(2)}) %collective-permute-start) | collective-permute-done | bytes 196640 | tf_op jit(solution)/shard_map/while/body/eval_jaxpr/ppermute | solution.py:27
  447.1 17.7 %conditional.2 = (bf16[16,6144]{1,0:T(8,128)(2,1)S(1)}) conditional(s32[]{:T(128)} %convert_element_type.52, () %tuple.48, (pred[]{:T(512)}, s32[]{:T(128)}, bf16[8,16,6144]{2,1,0:T(8,128)(2,1)}, bf16[16,6144]{1,0:T(8,128)(2,1)S(1)}, f32[6144]{0:T(1024)}, /*index=5*/s32[384]{0:T(512)S(1)}, bf16[192,64,128]{2,1,0:T(8,128)(2,1)}, s32[192]{0:T(256)S(1)}, ...), branch_computations={%region_4.4_spmd, %region_5.6_spmd} | conditional | flops 78352080 | bytes 19506548 | solution.py:108
  450.3 2.6 gather_fusion
  456.2 3.9 fusion.7
  461.5 2.3 convolution_bitcast_fusion
  467.8 6.7 %collective-permute-done = bf16[16,6144]{1,0:T(8,128)(2,1)S(1)} collective-permute-done((bf16[16,6144]{1,0:T(8,128)(2,1)S(1)}, bf16[16,6144]{1,0:T(8,128)(2,1)S(1)}, u32[]{:S(2)}, u32[]{:S(2)}) %collective-permute-start) | collective-permute-done | bytes 196640 | tf_op jit(solution)/shard_map/while/body/eval_jaxpr/ppermute | solution.py:27
  474.5 17.7 %conditional.2 = (bf16[16,6144]{1,0:T(8,128)(2,1)S(1)}) conditional(s32[]{:T(128)} %convert_element_type.52, () %tuple.48, (pred[]{:T(512)}, s32[]{:T(128)}, bf16[8,16,6144]{2,1,0:T(8,128)(2,1)}, bf16[16,6144]{1,0:T(8,128)(2,1)S(1)}, f32[6144]{0:T(1024)}, /*index=5*/s32[384]{0:T(512)S(1)}, bf16[192,64,128]{2,1,0:T(8,128)(2,1)}, s32[192]{0:T(256)S(1)}, ...), branch_computations={%region_4.4_spmd, %region_5.6_spmd} | conditional | flops 78352080 | bytes 19506548 | solution.py:108
  477.7 2.6 gather_fusion
  483.5 3.9 fusion.7
  488.8 2.3 convolution_bitcast_fusion
  495.1 4.6 collective-permute-done
  499.7 4.7 scatter_fusion
  (282 shorter events, 126.6 us)
Async XLA Ops:
  6.5 1.6 copy-start.4
  6.5 105.8 %all-gather.2.cloned.1.call-start = ((), (), s32[]{:S(2)}) async-start(), calls=%async_computation.1 | async-start | bytes 3342336 | tf_op jit(solution)/shard_map/all_gather | solution.py:46
  8.1 23.4 %copy-start.3 = (bf16[1,3,4096]{2,1,0:T(4,128)(2,1)S(1)}, bf16[1,3,4096]{2,1,0:T(4,128)(2,1)}, u32[]{:S(2)}) copy-start(bf16[1,3,4096]{2,1,0:T(4,128)(2,1)} %param.17) | copy-start | bytes 73732
  8.5 18.2 %collective-permute-start.1 = (bf16[3,64,128]{2,1,0:T(8,128)(2,1)S(1)}, bf16[3,64,128]{2,1,0:T(8,128)(2,1)S(1)}, u32[]{:S(2)}, u32[]{:S(2)}) collective-permute-start(bf16[3,64,128]{2,1,0:T(8,128)(2,1)S(1)} %reshape.129), channel_id=1, source_target_pairs={{0,16},{16,32},{32,48},{48,0},{1,17},{17,33},{33,49},{49,1},{2,18}... | collective-permute-start | bytes 147464 | tf_op jit(solution)/shard_map/ppermute | solution.py:35
  14.6 12.1 %collective-permute-start.2 = (bf16[3,64,128]{2,1,0:T(8,128)(2,1)S(1)}, bf16[3,64,128]{2,1,0:T(8,128)(2,1)S(1)}, u32[]{:S(2)}, u32[]{:S(2)}) collective-permute-start(bf16[3,64,128]{2,1,0:T(8,128)(2,1)S(1)} %reshape.129), channel_id=1, source_target_pairs={{0,32},{16,48},{32,0},{48,16},{1,33},{17,49},{33,1},{49,17},{2,34}... | collective-permute-start | bytes 147464 | tf_op jit(solution)/shard_map/ppermute | solution.py:35
  22.8 7.3 %collective-permute-start.3 = (bf16[3,64,128]{2,1,0:T(8,128)(2,1)S(1)}, bf16[3,64,128]{2,1,0:T(8,128)(2,1)S(1)}, u32[]{:S(2)}, u32[]{:S(2)}) collective-permute-start(bf16[3,64,128]{2,1,0:T(8,128)(2,1)S(1)} %reshape.129), channel_id=1, source_target_pairs={{0,48},{16,0},{32,16},{48,32},{1,49},{17,1},{33,17},{49,33},{2,50}... | collective-permute-start | bytes 147464 | tf_op jit(solution)/shard_map/ppermute | solution.py:35
  31.6 11.7 %collective-permute-start.4 = (bf16[96,128]{1,0:T(8,128)(2,1)S(1)}, bf16[96,128]{1,0:T(8,128)(2,1)S(1)}, u32[]{:S(2)}, u32[]{:S(2)}) collective-permute-start(bf16[96,128]{1,0:T(8,128)(2,1)S(1)} %reshape.131), channel_id=1, source_target_pairs={{0,16},{16,32},{32,48},{48,0},{1,17},{17,33},{33,49},{49,1},{2,18}... | collective-permute-start | bytes 73736 | tf_op jit(solution)/shard_map/ppermute | solution.py:35
  34.3 9.7 %collective-permute-start.5 = (bf16[96,128]{1,0:T(8,128)(2,1)S(1)}, bf16[96,128]{1,0:T(8,128)(2,1)S(1)}, u32[]{:S(2)}, u32[]{:S(2)}) collective-permute-start(bf16[96,128]{1,0:T(8,128)(2,1)S(1)} %reshape.131), channel_id=1, source_target_pairs={{0,32},{16,48},{32,0},{48,16},{1,33},{17,49},{33,1},{49,17},{2,34}... | collective-permute-start | bytes 73736 | tf_op jit(solution)/shard_map/ppermute | solution.py:35
  40.8 6.6 %collective-permute-start.6 = (bf16[96,128]{1,0:T(8,128)(2,1)S(1)}, bf16[96,128]{1,0:T(8,128)(2,1)S(1)}, u32[]{:S(2)}, u32[]{:S(2)}) collective-permute-start(bf16[96,128]{1,0:T(8,128)(2,1)S(1)} %reshape.131), channel_id=1, source_target_pairs={{0,48},{16,0},{32,16},{48,32},{1,49},{17,1},{33,17},{49,33},{2,50}... | collective-permute-start | bytes 73736 | tf_op jit(solution)/shard_map/ppermute | solution.py:35
  49.5 7.4 %copy-start.6 = (s32[160]{0:T(256)S(1)}, s32[160]{0:T(256)}, u32[]{:S(2)}) copy-start(s32[160]{0:T(256)} %param.12) | copy-start | bytes 1924
  49.5 50.7 %all-to-all-start = ((bf16[16,4,96,128]{3,2,1,0:T(8,128)(2,1)}), bf16[16,4,96,128]{3,2,1,0:T(8,128)(2,1)}, u32[]{:S(2)}, u32[]{:S(2)}) async-start(bf16[16,4,96,128]{3,2,1,0:T(8,128)(2,1)} %stack.51), calls=%async_computation | async-start | bytes 3145728 | tf_op jit(solution)/shard_map/all_to_all | solution.py:19
  62.3 2.8 copy-start.7
  62.3 3.1 copy-start.8
  62.3 3.3 copy-start.5
  112.4 8.6 %collective-permute-start = (bf16[16,6144]{1,0:T(8,128)(2,1)S(1)}, bf16[16,6144]{1,0:T(8,128)(2,1)S(1)}, u32[]{:S(2)}, u32[]{:S(2)}) collective-permute-start(bf16[16,6144]{1,0:T(8,128)(2,1)S(1)} %get-tuple-element.478), channel_id=1, source_target_pairs={{0,64},{64,128},{128,192},{192,256},{256,320},{320,384},{384,448},... | collective-permute-start | bytes 589832 | tf_op jit(solution)/shard_map/while/body/eval_jaxpr/ppermute | solution.py:27
  121.0 7.8 %collective-permute-start = (bf16[16,6144]{1,0:T(8,128)(2,1)S(1)}, bf16[16,6144]{1,0:T(8,128)(2,1)S(1)}, u32[]{:S(2)}, u32[]{:S(2)}) collective-permute-start(bf16[16,6144]{1,0:T(8,128)(2,1)S(1)} %get-tuple-element.478), channel_id=1, source_target_pairs={{0,64},{64,128},{128,192},{192,256},{256,320},{320,384},{384,448},... | collective-permute-start | bytes 589832 | tf_op jit(solution)/shard_map/while/body/eval_jaxpr/ppermute | solution.py:27
  128.8 7.6 %collective-permute-start = (bf16[16,6144]{1,0:T(8,128)(2,1)S(1)}, bf16[16,6144]{1,0:T(8,128)(2,1)S(1)}, u32[]{:S(2)}, u32[]{:S(2)}) collective-permute-start(bf16[16,6144]{1,0:T(8,128)(2,1)S(1)} %get-tuple-element.478), channel_id=1, source_target_pairs={{0,64},{64,128},{128,192},{192,256},{256,320},{320,384},{384,448},... | collective-permute-start | bytes 589832 | tf_op jit(solution)/shard_map/while/body/eval_jaxpr/ppermute | solution.py:27
  136.4 7.6 %collective-permute-start = (bf16[16,6144]{1,0:T(8,128)(2,1)S(1)}, bf16[16,6144]{1,0:T(8,128)(2,1)S(1)}, u32[]{:S(2)}, u32[]{:S(2)}) collective-permute-start(bf16[16,6144]{1,0:T(8,128)(2,1)S(1)} %get-tuple-element.478), channel_id=1, source_target_pairs={{0,64},{64,128},{128,192},{192,256},{256,320},{320,384},{384,448},... | collective-permute-start | bytes 589832 | tf_op jit(solution)/shard_map/while/body/eval_jaxpr/ppermute | solution.py:27
  144.0 7.7 %collective-permute-start = (bf16[16,6144]{1,0:T(8,128)(2,1)S(1)}, bf16[16,6144]{1,0:T(8,128)(2,1)S(1)}, u32[]{:S(2)}, u32[]{:S(2)}) collective-permute-start(bf16[16,6144]{1,0:T(8,128)(2,1)S(1)} %get-tuple-element.478), channel_id=1, source_target_pairs={{0,64},{64,128},{128,192},{192,256},{256,320},{320,384},{384,448},... | collective-permute-start | bytes 589832 | tf_op jit(solution)/shard_map/while/body/eval_jaxpr/ppermute | solution.py:27
  151.7 9.7 %collective-permute-start = (bf16[16,6144]{1,0:T(8,128)(2,1)S(1)}, bf16[16,6144]{1,0:T(8,128)(2,1)S(1)}, u32[]{:S(2)}, u32[]{:S(2)}) collective-permute-start(bf16[16,6144]{1,0:T(8,128)(2,1)S(1)} %get-tuple-element.478), channel_id=1, source_target_pairs={{0,64},{64,128},{128,192},{192,256},{256,320},{320,384},{384,448},... | collective-permute-start | bytes 589832 | tf_op jit(solution)/shard_map/while/body/eval_jaxpr/ppermute | solution.py:27
  161.4 121.6 %collective-permute-start = (bf16[16,6144]{1,0:T(8,128)(2,1)S(1)}, bf16[16,6144]{1,0:T(8,128)(2,1)S(1)}, u32[]{:S(2)}, u32[]{:S(2)}) collective-permute-start(bf16[16,6144]{1,0:T(8,128)(2,1)S(1)} %get-tuple-element.478), channel_id=1, source_target_pairs={{0,64},{64,128},{128,192},{192,256},{256,320},{320,384},{384,448},... | collective-permute-start | bytes 589832 | tf_op jit(solution)/shard_map/while/body/eval_jaxpr/ppermute | solution.py:27
  284.1 0.7 copy-start.1
  299.7 0.9 copy-start.2
  300.7 9.7 %collective-permute-start = (bf16[16,6144]{1,0:T(8,128)(2,1)S(1)}, bf16[16,6144]{1,0:T(8,128)(2,1)S(1)}, u32[]{:S(2)}, u32[]{:S(2)}) collective-permute-start(bf16[16,6144]{1,0:T(8,128)(2,1)S(1)} %get-tuple-element.478), channel_id=1, source_target_pairs={{0,64},{64,128},{128,192},{192,256},{256,320},{320,384},{384,448},... | collective-permute-start | bytes 589832 | tf_op jit(solution)/shard_map/while/body/eval_jaxpr/ppermute | solution.py:27
  311.5 0.7 copy-start.1
  327.1 0.9 copy-start.2
  328.1 9.7 %collective-permute-start = (bf16[16,6144]{1,0:T(8,128)(2,1)S(1)}, bf16[16,6144]{1,0:T(8,128)(2,1)S(1)}, u32[]{:S(2)}, u32[]{:S(2)}) collective-permute-start(bf16[16,6144]{1,0:T(8,128)(2,1)S(1)} %get-tuple-element.478), channel_id=1, source_target_pairs={{0,64},{64,128},{128,192},{192,256},{256,320},{320,384},{384,448},... | collective-permute-start | bytes 589832 | tf_op jit(solution)/shard_map/while/body/eval_jaxpr/ppermute | solution.py:27
  338.8 0.7 copy-start.1
  354.4 0.9 copy-start.2
  355.4 9.7 %collective-permute-start = (bf16[16,6144]{1,0:T(8,128)(2,1)S(1)}, bf16[16,6144]{1,0:T(8,128)(2,1)S(1)}, u32[]{:S(2)}, u32[]{:S(2)}) collective-permute-start(bf16[16,6144]{1,0:T(8,128)(2,1)S(1)} %get-tuple-element.478), channel_id=1, source_target_pairs={{0,64},{64,128},{128,192},{192,256},{256,320},{320,384},{384,448},... | collective-permute-start | bytes 589832 | tf_op jit(solution)/shard_map/while/body/eval_jaxpr/ppermute | solution.py:27
  366.2 0.7 copy-start.1
  381.8 0.9 copy-start.2
  382.8 9.7 %collective-permute-start = (bf16[16,6144]{1,0:T(8,128)(2,1)S(1)}, bf16[16,6144]{1,0:T(8,128)(2,1)S(1)}, u32[]{:S(2)}, u32[]{:S(2)}) collective-permute-start(bf16[16,6144]{1,0:T(8,128)(2,1)S(1)} %get-tuple-element.478), channel_id=1, source_target_pairs={{0,64},{64,128},{128,192},{192,256},{256,320},{320,384},{384,448},... | collective-permute-start | bytes 589832 | tf_op jit(solution)/shard_map/while/body/eval_jaxpr/ppermute | solution.py:27
  393.5 0.7 copy-start.1
  409.1 0.9 copy-start.2
  410.1 9.7 %collective-permute-start = (bf16[16,6144]{1,0:T(8,128)(2,1)S(1)}, bf16[16,6144]{1,0:T(8,128)(2,1)S(1)}, u32[]{:S(2)}, u32[]{:S(2)}) collective-permute-start(bf16[16,6144]{1,0:T(8,128)(2,1)S(1)} %get-tuple-element.478), channel_id=1, source_target_pairs={{0,64},{64,128},{128,192},{192,256},{256,320},{320,384},{384,448},... | collective-permute-start | bytes 589832 | tf_op jit(solution)/shard_map/while/body/eval_jaxpr/ppermute | solution.py:27
  420.9 0.7 copy-start.1
  436.5 0.9 copy-start.2
  437.4 9.7 %collective-permute-start = (bf16[16,6144]{1,0:T(8,128)(2,1)S(1)}, bf16[16,6144]{1,0:T(8,128)(2,1)S(1)}, u32[]{:S(2)}, u32[]{:S(2)}) collective-permute-start(bf16[16,6144]{1,0:T(8,128)(2,1)S(1)} %get-tuple-element.478), channel_id=1, source_target_pairs={{0,64},{64,128},{128,192},{192,256},{256,320},{320,384},{384,448},... | collective-permute-start | bytes 589832 | tf_op jit(solution)/shard_map/while/body/eval_jaxpr/ppermute | solution.py:27
  448.2 0.7 copy-start.1
  463.8 0.9 copy-start.2
  464.8 9.7 %collective-permute-start = (bf16[16,6144]{1,0:T(8,128)(2,1)S(1)}, bf16[16,6144]{1,0:T(8,128)(2,1)S(1)}, u32[]{:S(2)}, u32[]{:S(2)}) collective-permute-start(bf16[16,6144]{1,0:T(8,128)(2,1)S(1)} %get-tuple-element.478), channel_id=1, source_target_pairs={{0,64},{64,128},{128,192},{192,256},{256,320},{320,384},{384,448},... | collective-permute-start | bytes 589832 | tf_op jit(solution)/shard_map/while/body/eval_jaxpr/ppermute | solution.py:27
  475.6 0.7 copy-start.1
  491.2 0.9 copy-start.2
  492.1 7.6 %collective-permute-start = (bf16[16,6144]{1,0:T(8,128)(2,1)S(1)}, bf16[16,6144]{1,0:T(8,128)(2,1)S(1)}, u32[]{:S(2)}, u32[]{:S(2)}) collective-permute-start(bf16[16,6144]{1,0:T(8,128)(2,1)S(1)} %get-tuple-element.478), channel_id=1, source_target_pairs={{0,64},{64,128},{128,192},{192,256},{256,320},{320,384},{384,448},... | collective-permute-start | bytes 589832 | tf_op jit(solution)/shard_map/while/body/eval_jaxpr/ppermute | solution.py:27
  504.4 1.3 copy-start
Sparse Core Ops, SparseCore 0:
  31.7 56.9 all-gather.1
